TPU v7x, 128 devices: a whole 4x4x4 slice. The times are simulated.
128 devices in a mesh: gx: 4 (over z), gy: 32 (over y, x, core).
Axes of the slice: x: 4, y: 4, z: 4, core: 2. Of those that a mesh axis runs over, the one named last changes fastest.
Arguments:
- tokens: bfloat16 [32768, 1664], P('gy', 'gx'), may hold values from -6 to 6
- segment_ids: int32 [32768], P('gy'), may hold values from 0 to 1023, as said below
- first_gain: float32 [1664], replicated, may hold values from 0.5 to 2
- first_bias: float32 [1664], replicated, may hold values from -3 to 3
- query_key_value: bfloat16 [3, 1664, 1664], P(None, 'gy', 'gx'), may hold values from -0.15625 to 0.15625
- project_out: bfloat16 [1664, 1664], P('gx', 'gy'), may hold values from -0.15625 to 0.15625
- second_gain: float32 [1664], replicated, may hold values from 0.5 to 2
- second_bias: float32 [1664], replicated, may hold values from -3 to 3
- up_weight: bfloat16 [1664, 8192], P('gy', 'gx'), may hold values from -0.15625 to 0.15625
- down_weight: bfloat16 [8192, 1664], P('gx', 'gy'), may hold values from -0.0625 to 0.0625
- final_gain: float32 [1664], replicated, may hold values from 0.5 to 2
- final_bias: float32 [1664], replicated, may hold values from -3 to 3
- merge_weight: bfloat16 [4, 1664, 1664], P(None, 'gx', 'gy'), may hold values from -0.078125 to 0.078125
- owners: int32 [8192, 1], P('gy'), may hold values from 0 to 31; in each aligned block of 256 rows (0 to 255, 256 to 511, ...) at most 16 rows name the same one
Outputs:
- delivered: bfloat16 [32, 32, 16, 1664], P('gy', None, None, 'gx')
Inputs may be any that keep to these rules, and one draw needn't show every extreme that they name: `segment_ids`: each segment is a run of whole units of 32 consecutive tokens that lies inside one aligned block of 1024 tokens; ids never fall along the tokens and differ between segments. `owners`: in each aligned block of 256 rows (the merged tokens of one index of gy), no owner is named by more than 16 rows.
All inputs are finite; a program needn't handle non-finite values.
Results may differ from a plain program's by a relative error of at most 0.02.
Values may be sent and summed in bfloat16 or wider, within the bound.
No kernel may reach another device: no remote copies, remote signals or barrier semaphores. Data moves between devices by JAX's collectives and lax.ppermute only.
A program may use at most 128 MiB of HBM per device.

v0:
```python
import jax
import jax.numpy as jnp
from jax import lax
from jax.sharding import PartitionSpec as P

HEAD = 104
IMG_W = 16
EPSILON = 1e-06


def normalize_rows(values, gain, bias):
    values = values.astype(jnp.float32)
    center = values - jnp.mean(values, axis=-1, keepdims=True)
    spread = jnp.mean(center * center, axis=-1, keepdims=True)
    return center * lax.rsqrt(spread + EPSILON) * gain + bias


def normalize_from_sums(values, sums, features, gain, bias):
    values = values.astype(jnp.float32)
    row_mean = sums[0] / features
    spread = sums[1] / features - row_mean * row_mean
    return (values - row_mean[:, None]) * lax.rsqrt(spread[:, None] + EPSILON) * gain + bias


def own_slice(vector, width):
    return lax.dynamic_slice_in_dim(vector, lax.axis_index("gx") * width, width, 0)


def row_sums(values):
    values = values.astype(jnp.float32)
    return (jnp.sum(values, axis=-1), jnp.sum(values * values, axis=-1))


def local_attention(qkv, segment_ids):
    tok_rows = qkv.shape[1]
    head_count = qkv.shape[2] // HEAD
    queries = qkv[0].reshape(tok_rows, head_count, HEAD)
    key_rows = qkv[1].reshape(tok_rows, head_count, HEAD)
    value_rows = qkv[2].reshape(tok_rows, head_count, HEAD)
    query_block = min(512, tok_rows)

    def one_block(index):
        first_query = index * query_block
        query_part = lax.dynamic_slice_in_dim(queries, first_query, query_block, 0)
        query_ids = lax.dynamic_slice_in_dim(segment_ids, first_query, query_block, 0)
        scores = jnp.einsum(
            "qhe,khe->hqk", query_part, key_rows, preferred_element_type=jnp.float32
        ) * HEAD ** (-0.5)
        same_segment = query_ids[None, :, None] == segment_ids[None, None, :]
        scores = jnp.where(same_segment, scores, -1e30)
        highest = jnp.max(scores, axis=-1, keepdims=True)
        raised = jnp.exp(scores - highest)
        shares = (raised / jnp.sum(raised, axis=-1, keepdims=True)).astype(jnp.bfloat16)
        return jnp.einsum(
            "hqk,khe->qhe", shares, value_rows, preferred_element_type=jnp.float32
        ).astype(jnp.bfloat16)

    blocks = lax.map(one_block, jnp.arange(tok_rows // query_block, dtype=jnp.int32))
    return blocks.reshape(tok_rows, head_count * HEAD)


def body(
    tokens,
    segment_ids,
    first_gain,
    first_bias,
    query_key_value,
    project_out,
    second_gain,
    second_bias,
    up_weight,
    down_weight,
    final_gain,
    final_bias,
    merge_weight,
    owners,
):
    tok_rows = tokens.shape[0]
    feature_cols = tokens.shape[1]
    features = feature_cols * lax.axis_size("gx")
    full_rows = lax.all_gather(tokens, "gx", axis=1, tiled=True)
    normed = normalize_rows(full_rows, first_gain, first_bias).astype(jnp.bfloat16)
    columns = normed
    qkv = jnp.einsum(
        "td,kdc->ktc",
        columns,
        lax.all_gather(query_key_value, "gy", axis=1, tiled=True),
        preferred_element_type=jnp.float32,
    ).astype(jnp.bfloat16)
    attended = local_attention(qkv, segment_ids)
    out_terms = jnp.dot(
        attended,
        lax.all_gather(project_out, "gy", axis=1, tiled=True),
        preferred_element_type=jnp.float32,
    )
    attn_share = lax.psum_scatter(
        out_terms.astype(jnp.bfloat16), "gx", scatter_dimension=1, tiled=True
    ).astype(jnp.float32)
    first_resid = (tokens.astype(jnp.float32) + attn_share).astype(jnp.bfloat16)
    resid_rows = lax.all_gather(first_resid, "gx", axis=1, tiled=True)
    second_normed = normalize_rows(resid_rows, second_gain, second_bias).astype(jnp.bfloat16)
    columns = second_normed
    upper = jnp.dot(
        columns,
        lax.all_gather(up_weight, "gy", axis=0, tiled=True),
        preferred_element_type=jnp.float32,
    )
    hidden = jax.nn.gelu(upper, approximate=False).astype(jnp.bfloat16)
    down_terms = jnp.dot(
        hidden,
        lax.all_gather(down_weight, "gy", axis=1, tiled=True),
        preferred_element_type=jnp.float32,
    )
    mlp_share = lax.psum_scatter(
        down_terms.astype(jnp.bfloat16), "gx", scatter_dimension=1, tiled=True
    ).astype(jnp.float32)
    second_resid = (first_resid.astype(jnp.float32) + mlp_share).astype(jnp.bfloat16)
    post_sums = lax.psum(row_sums(second_resid), "gx")
    final_normed = normalize_from_sums(
        second_resid,
        post_sums,
        features,
        own_slice(final_gain, feature_cols),
        own_slice(final_bias, feature_cols),
    ).astype(jnp.bfloat16)
    merged_rows = tok_rows // 4
    grouped = (
        final_normed.reshape(tok_rows // (2 * IMG_W), 2, IMG_W // 2, 2, feature_cols)
        .transpose(0, 2, 1, 3, 4)
        .reshape(merged_rows, 4, feature_cols)
    )
    merge_terms = jnp.einsum(
        "pkf,kfc->pc",
        grouped,
        lax.all_gather(merge_weight, "gy", axis=2, tiled=True),
        preferred_element_type=jnp.float32,
    )
    projected = lax.psum_scatter(
        merge_terms.astype(jnp.bfloat16), "gx", scatter_dimension=1, tiled=True
    )
    owner_count = lax.axis_size("gy")
    capacity = max(2, 2 * merged_rows // owner_count)
    owner_col = owners[:, 0]
    one_hot = (owner_col[:, None] == jnp.arange(owner_count, dtype=jnp.int32)[None, :]).astype(
        jnp.int32
    )
    slot_rank = jnp.sum((jnp.cumsum(one_hot, axis=0) - 1) * one_hot, axis=1)
    outgoing = (
        jnp.zeros((owner_count, capacity, feature_cols), jnp.bfloat16)
        .at[owner_col, slot_rank]
        .set(projected)
    )
    arrived = lax.all_to_all(outgoing, "gy", split_axis=0, concat_axis=0, tiled=True)
    return arrived.reshape(1, owner_count, capacity, feature_cols)


def solution(mesh):
    in_specs = (
        P("gy", "gx"),
        P("gy"),
        P(),
        P(),
        P(None, "gy", "gx"),
        P("gx", "gy"),
        P(),
        P(),
        P("gy", "gx"),
        P("gx", "gy"),
        P(),
        P(),
        P(None, "gx", "gy"),
        P("gy", None),
    )
    out_specs = P("gy", None, None, "gx")
    return jax.shard_map(body, mesh=mesh, in_specs=in_specs, out_specs=out_specs, check_vma=False)
```

profile of v0, /device:TPU:1, one launch (start us, length us, event | category | flops | bytes accessed | tf_op | source)
XLA Modules:
  0.0 590.1 jit_solution(16521097210101806304)
XLA Ops:
  9.9 46.5 %all-gather.19.cloned.1.call-done = bf16[32,52,416]{2,1,0:T(8,128)(2,1)} async-done(((bf16[1,52,416]{2,1,0:T(8,128)(2,1)}), bf16[32,52,416]{2,1,0:T(8,128)(2,1)}) %all-gather.19.cloned.1.call-update) | async-done | bytes 1384464 | tf_op jit(solution)/shard_map/all_gather | solution.py:93
  60.2 38.4 %all-gather.11.cloned.1.call-done = bf16[1024,1664]{0,1:T(8,128)(2,1)} async-done(((bf16[1024,416]{0,1:T(8,128)(2,1)}), bf16[1024,1664]{0,1:T(8,128)(2,1)}) %all-gather.11.cloned.1.call-update) | async-done | bytes 3407888 | tf_op jit(solution)/shard_map/all_gather | solution.py:81
  104.3 47.0 %all-gather.13.cloned.1.call-done = bf16[3,1664,416]{2,0,1:T(4,128)(2,1)} async-done(((bf16[3,52,416]{2,0,1:T(4,128)(2,1)}), bf16[3,1664,416]{2,0,1:T(4,128)(2,1)}) %all-gather.13.cloned.1.call-update) | async-done | bytes 4153360 | tf_op jit(solution)/shard_map/all_gather | solution.py:87
  151.3 8.7 %convert_bitcast_fusion = bf16[3,1024,416]{1,2,0:T(8,128)(2,1)S(1)} fusion(bf16[3,1664,416]{2,0,1:T(4,128)(2,1)} %all-gather.13.cloned.1.call-done, bf16[1024,1664]{0,1:T(8,128)(2,1)S(1)} %copy-done.1, f32[1664]{0:T(1024)S(1)} %copy-done.7, f32[1664]{0:T(1024)S(1)} %copy-done.8, f32[1024]{0:T(1024)S(1)} %add_rsqrt_fusion.2, ...), kind=kOutput, calls=%fused_computation.79 | convolution fusion | flops 4264525824 | bytes 10138624 | tf_op jit(solution)/shard_map/td,kdc->ktc/dot_general | solution.py:84
  161.5 30.1 %while.10 = (s32[]{:T(128)}, bf16[2,512,4,104]{1,3,2,0:T(8,128)(2,1)}, s32[2]{0:T(128)S(1)}, s32[1024]{0:T(1024)S(1)}, bf16[1024,4,104]{0,2,1:T(8,128)(2,1)}, /*...) while((s32[]{:T(128)}, ...), condition=%wide.region_8.9_spmd, body=%wide.region_5.8_spmd.sunk | while | flops 885736448 | bytes 20409008 | solution.py:58
  163.4 7.6 %fusion.157 = (f32[4,512]{1,0:T(4,128)S(1)}, f32[4,512,1024]{2,1,0:T(8,128)}) fusion(pred[512,1024]{1,0:T(8,128)(4,1)S(1)} %broadcast_compare_fusion.2, bf16[1024,4,104]{0,2,1:T(8,128)(2,1)} %get-tuple-element.142, bf16[1024,4,104]{0,2,1:T(8,128)(2,1)} %get-tuple-element.141, s32[]{:T(128)S(6)} %select_n.48), kind=kOutput, calls=%fused_computation.137.clone.1 | convolution fusion | flops 444597248 | bytes 10199044 | tf_op jit(solution)/shard_map/while/body/eval_jaxpr/sub | solution.py:52
  171.0 5.7 fusion.158
  178.3 7.6 %fusion.157 = (f32[4,512]{1,0:T(4,128)S(1)}, f32[4,512,1024]{2,1,0:T(8,128)}) fusion(pred[512,1024]{1,0:T(8,128)(4,1)S(1)} %broadcast_compare_fusion.2, bf16[1024,4,104]{0,2,1:T(8,128)(2,1)} %get-tuple-element.142, bf16[1024,4,104]{0,2,1:T(8,128)(2,1)} %get-tuple-element.141, s32[]{:T(128)S(6)} %select_n.48), kind=kOutput, calls=%fused_computation.137.clone.1 | convolution fusion | flops 444597248 | bytes 10199044 | tf_op jit(solution)/shard_map/while/body/eval_jaxpr/sub | solution.py:52
  185.9 5.7 fusion.158
  198.7 38.0 %reduce-scatter.4.cloned.1.call-done = bf16[1024,416]{0,1:T(8,128)(2,1)} async-done(((bf16[1024,1664]{0,1:T(8,128)(2,1)}), bf16[1024,416]{0,1:T(8,128)(2,1)}) %reduce-scatter.4.cloned.1.call-update) | async-done | bytes 851984 | tf_op jit(solution)/shard_map/reduce_scatter | solution.py:96
  239.3 50.2 %all-gather.21.cloned.1.call-done = bf16[32,52,2048]{2,1,0:T(8,128)(2,1)} async-done(((bf16[1,52,2048]{2,1,0:T(8,128)(2,1)}), bf16[32,52,2048]{2,1,0:T(8,128)(2,1)}) %all-gather.21.cloned.1.call-update) | async-done | bytes 6815760 | tf_op jit(solution)/shard_map/all_gather | solution.py:105
  289.5 8.6 %reshape.127 = bf16[1664,2048]{1,0:T(8,128)(2,1)} reshape(bf16[32,52,2048]{2,1,0:T(8,128)(2,1)} %all-gather.21.cloned.1.call-done) | data formatting | bytes 13631488
  298.1 43.3 %all-gather.23.cloned.1.call-done = bf16[32,52,2048]{2,1,0:T(8,128)(2,1)} async-done(((bf16[1,52,2048]{2,1,0:T(8,128)(2,1)}), bf16[32,52,2048]{2,1,0:T(8,128)(2,1)}) %all-gather.23.cloned.1.call-update) | async-done | bytes 6815760 | tf_op jit(solution)/shard_map/all_gather | solution.py:111
  341.5 8.8 %reshape.129 = bf16[1664,2048]{1,0:T(8,128)(2,1)} reshape(bf16[32,52,2048]{2,1,0:T(8,128)(2,1)} %all-gather.23.cloned.1.call-done) | data formatting | bytes 13631488
  350.3 33.4 %all-gather.15.cloned.1.call-done = bf16[1024,1664]{0,1:T(8,128)(2,1)} async-done(((bf16[1024,416]{0,1:T(8,128)(2,1)}), bf16[1024,1664]{0,1:T(8,128)(2,1)}) %all-gather.15.cloned.1.call-update) | async-done | bytes 3407888 | tf_op jit(solution)/shard_map/all_gather | solution.py:100
  389.5 29.4 %fusion.147 = bf16[1024,2048]{1,0:T(8,128)(2,1)S(1)} fusion(bf16[1664,2048]{1,0:T(8,128)(2,1)} %reshape.127, bf16[1024,1664]{0,1:T(8,128)(2,1)S(1)} %copy-done.2, f32[1664]{0:T(1024)S(1)} %copy-done.9, f32[1664]{0:T(1024)S(1)} %copy-done.10, f32[1024]{0:T(1024)S(1)} %add_rsqrt_fusion.1, f32[1024]{0:T(1024)S(1)} %broadcast_multiply_fusion.1), kind=kOutput, calls=%fused_computation.29.clone.clone.clone.clone.1 | convolution fusion | flops 7125860352 | bytes 14439424 | tf_op jit(solution)/shard_map/dot_general | solution.py:103
  419.0 8.7 %fusion.52 = bf16[1024,1664]{0,1:T(8,128)(2,1)} fusion(bf16[1664,2048]{1,0:T(8,128)(2,1)S(1)} %bitcast.78, bf16[1024,2048]{1,0:T(8,128)(2,1)S(1)} %fusion.147), kind=kOutput, calls=%fused_computation.62 | convolution fusion | flops 6981025792 | bytes 14417920 | tf_op jit(solution)/shard_map/dot_general | solution.py:109
  430.1 38.6 %reduce-scatter.6.cloned.1.call-done = bf16[1024,416]{0,1:T(8,128)(2,1)} async-done(((bf16[1024,1664]{0,1:T(8,128)(2,1)}), bf16[1024,416]{0,1:T(8,128)(2,1)}) %reduce-scatter.6.cloned.1.call-update) | async-done | bytes 851984 | tf_op jit(solution)/shard_map/reduce_scatter | solution.py:114
  470.2 6.6 %all-reduce = (f32[1024]{0:T(1024)S(1)}, f32[1024]{0:T(1024)S(1)}) all-reduce(f32[1024]{0:T(1024)S(1)} %get-tuple-element.44, f32[1024]{0:T(1024)S(1)} %get-tuple-element.43), channel_id=1, replica_groups=mesh['gx'=4,'gy'=32] {'gx'}, use_global_device_ids=true, to_apply=%region_16.17 | all-reduce | flops 2048 | bytes 16384 | tf_op jit(solution)/shard_map/psum | solution.py:118
  479.9 40.9 %all-gather.17.cloned.1.call-done = bf16[4,416,1664]{1,0,2:T(4,128)(2,1)} async-done(((bf16[4,416,52]{1,0,2:T(4,128)(2,1)}), bf16[4,416,1664]{1,0,2:T(4,128)(2,1)}) %all-gather.17.cloned.1.call-update) | async-done | bytes 5537808 | tf_op jit(solution)/shard_map/all_gather | solution.py:135
  520.8 6.3 %fusion.78 = bf16[256,1664]{0,1:T(8,128)(2,1)} fusion(bf16[256,4,416]{2,0,1:T(8,128)(2,1)S(1)} %bitcast.82, bf16[4,416,1664]{1,0,2:T(4,128)(2,1)} %all-gather.17.cloned.1.call-done), kind=kOutput, calls=%fused_computation.75 | convolution fusion | flops 1418100736 | bytes 7241728 | tf_op jit(solution)/shard_map/pkf,kfc->pc/dot_general | solution.py:132
  528.1 19.4 %reduce-scatter.8.cloned.1.call-done = bf16[256,416]{0,1:T(8,128)(2,1)} async-done(((bf16[256,1664]{0,1:T(8,128)(2,1)}), bf16[256,416]{0,1:T(8,128)(2,1)}) %reduce-scatter.8.cloned.1.call-update) | async-done | bytes 213008 | tf_op jit(solution)/shard_map/reduce_scatter | solution.py:138
  548.7 13.6 %scatter_fusion = bf16[32,16,416]{2,1,0:T(8,128)(2,1)S(1)} fusion(bf16[32,16,416]{2,1,0:T(8,128)(2,1)S(1)} %broadcast_in_dim.24, s32[256]{0:T(256)S(1)} %bitcast.76, bf16[256,416]{1,0:T(8,128)(2,1)S(1)} %copy.35), kind=kCustom, calls=%fused_computation | custom fusion | bytes 641024 | tf_op jit(solution)/shard_map/scatter | solution.py:151
  562.3 20.0 %all_to_all.5 = bf16[32,16,416]{2,1,0:T(8,128)(2,1)S(1)} all-to-all(bf16[32,16,416]{2,1,0:T(8,128)(2,1)S(1)} %scatter_fusion), channel_id=1, replica_groups=mesh['gx'=4,'gy'=32] {'gy'}, dimensions={0} | all-to-all | bytes 851968 | tf_op jit(solution)/shard_map/all_to_all | solution.py:153
  (88 shorter events, 41.5 us)
Async XLA Ops:
  6.5 144.8 %copy-start.8 = (f32[1664]{0:T(1024)S(1)}, f32[1664]{0:T(1024)}, u32[]{:S(2)}) copy-start(f32[1664]{0:T(1024)} %param.18) | copy-start | bytes 19972
  6.5 144.8 %copy-start.7 = (f32[1664]{0:T(1024)S(1)}, f32[1664]{0:T(1024)}, u32[]{:S(2)}) copy-start(f32[1664]{0:T(1024)} %param.19) | copy-start | bytes 19972
  6.5 49.8 %all-gather.19.cloned.1.call-start = ((), (), s32[]{:S(2)}) async-start(), calls=%async_computation.11 | async-start | bytes 1892352 | tf_op jit(solution)/shard_map/all_gather | solution.py:93
  7.3 91.4 %all-gather.11.cloned.1.call-start = ((), (), s32[]{:S(2)}) async-start(), calls=%async_computation.4 | async-start | bytes 4259840 | tf_op jit(solution)/shard_map/all_gather | solution.py:81
  8.0 143.3 %all-gather.13.cloned.1.call-start = ((), (), s32[]{:S(2)}) async-start(), calls=%async_computation.5 | async-start | bytes 7028736 | tf_op jit(solution)/shard_map/all_gather | solution.py:87
  9.8 227.0 %reduce-scatter.4.cloned.1.call-start = ((), (), s32[]{:S(2)}) async-start(), calls=%async_computation.6 | async-start | bytes 4259840 | tf_op jit(solution)/shard_map/reduce_scatter | solution.py:96
  98.7 52.6 %copy-start.1 = (bf16[1024,1664]{0,1:T(8,128)(2,1)S(1)}, bf16[1024,1664]{0,1:T(8,128)(2,1)}, u32[]{:S(2)}) copy-start(bf16[1024,1664]{0,1:T(8,128)(2,1)} %all-gather.11.cloned.1.call-done) | copy-start | bytes 10223620
  104.3 57.2 %copy-start.5 = (s32[1024]{0:T(1024)S(1)}, s32[1024]{0:T(1024)}, u32[]{:S(2)}) copy-start(s32[1024]{0:T(1024)} %param.17) | copy-start | bytes 12292
  161.5 32.3 %copy-start.4 = (bf16[1664,416]{1,0:T(8,128)(2,1)S(1)}, bf16[1664,416]{1,0:T(8,128)(2,1)}, u32[]{:S(2)}) copy-start(bf16[1664,416]{1,0:T(8,128)(2,1)} %reshape.125) | copy-start | bytes 4153348
  193.8 42.9 %copy-start.3 = (bf16[1024,416]{0,1:T(8,128)(2,1)S(1)}, bf16[1024,416]{0,1:T(8,128)(2,1)}, u32[]{:S(2)}) copy-start(bf16[1024,416]{0,1:T(8,128)(2,1)} %param.16) | copy-start | bytes 2555908
  197.5 92.0 %all-gather.21.cloned.1.call-start = ((), (), s32[]{:S(2)}) async-start(), calls=%async_computation.12 | async-start | bytes 7569408 | tf_op jit(solution)/shard_map/all_gather | solution.py:105
  198.1 143.3 %all-gather.23.cloned.1.call-start = ((), (), s32[]{:S(2)}) async-start(), calls=%async_computation.13 | async-start | bytes 7569408 | tf_op jit(solution)/shard_map/all_gather | solution.py:111
  198.7 185.0 %all-gather.15.cloned.1.call-start = ((), (), s32[]{:S(2)}) async-start(), calls=%async_computation.7 | async-start | bytes 4259840 | tf_op jit(solution)/shard_map/all_gather | solution.py:100
  239.2 229.5 %reduce-scatter.6.cloned.1.call-start = ((), (), s32[]{:S(2)}) async-start(), calls=%async_computation.8 | async-start | bytes 4259840 | tf_op jit(solution)/shard_map/reduce_scatter | solution.py:114
  350.2 39.3 %copy-start.9 = (f32[1664]{0:T(1024)S(1)}, f32[1664]{0:T(1024)}, u32[]{:S(2)}) copy-start(f32[1664]{0:T(1024)} %param.23) | copy-start | bytes 19972
  350.2 39.3 %copy-start.10 = (f32[1664]{0:T(1024)S(1)}, f32[1664]{0:T(1024)}, u32[]{:S(2)}) copy-start(f32[1664]{0:T(1024)} %param.22) | copy-start | bytes 19972
  383.7 5.9 copy-start.2
  386.4 32.5 %slice-start = ((s8[6815744]{0:T(1024)(128)(4,1)}), s8[4194304]{0:T(1024)(128)(4,1)S(1)}, s32[]{:S(2)}) async-start(s8[6815744]{0:T(1024)(128)(4,1)} %bitcast.77), calls=%async_computation.14 | async-start | bytes 8388608
  389.5 29.4 %slice-start.1 = ((s8[6815744]{0:T(1024)(128)(4,1)}), s8[2621440]{0:T(1024)(128)(4,1)S(1)}, s32[]{:S(2)}) async-start(s8[6815744]{0:T(1024)(128)(4,1)} %bitcast.77), calls=%async_computation.15 | async-start | bytes 5242880
  419.0 49.7 %copy-start = (bf16[1024,416]{0,1:T(8,128)(2,1)S(1)}, bf16[1024,416]{0,1:T(8,128)(2,1)}, u32[]{:S(2)}) copy-start(bf16[1024,416]{0,1:T(8,128)(2,1)} %add_convert_fusion.1) | copy-start | bytes 2555908
  427.7 93.0 %all-gather.17.cloned.1.call-start = ((), (), s32[]{:S(2)}) async-start(), calls=%async_computation.9 | async-start | bytes 7028736 | tf_op jit(solution)/shard_map/all_gather | solution.py:135
  428.5 119.1 %reduce-scatter.8.cloned.1.call-start = ((), (), s32[]{:S(2)}) async-start(), calls=%async_computation.10 | async-start | bytes 1064960 | tf_op jit(solution)/shard_map/reduce_scatter | solution.py:138
  520.7 6.4 %copy-start.6 = (s32[256,1]{0,1:T(1,128)S(1)}, s32[256,1]{0,1:T(1,128)}, u32[]{:S(2)}) copy-start(s32[256,1]{0,1:T(1,128)} %param.29) | copy-start | bytes 3076
Sparse Core Ops, SparseCore 0:
  9.6 46.7 all-gather.18
  58.0 40.5 all-gather.10
  100.9 50.3 all-gather.12
  197.6 39.0 reduce-scatter.3
  238.8 50.6 all-gather.20
  291.6 49.7 all-gather.22
  343.1 40.5 all-gather.14
  427.9 40.7 reduce-scatter.5
  471.0 49.7 all-gather.16
  527.2 20.2 reduce-scatter.7
where the time goes:
time: 598 us; the launch traced here: 590 us
  waiting for transfers between devices  399 us (67%)
  matrix products  83.4 us (14%)
  local copies, waits for them, and re-layouts  46.7 us (8%)
  blocking collectives  26.6 us (4%)
  other arithmetic  18.5 us (3%)
  between operations  14 us (2%)
    all_gather x1, waiting for transfers between devices, body(): lax.all_gather(up_weight, 'gy', axis=0, tiled=True)  50.2 us
    all_gather x1, waiting for transfers between devices, body(): lax.all_gather(query_key_value, 'gy', axis=1, tiled=True)  47 us
    all_gather x1, waiting for transfers between devices, body(): lax.all_gather(project_out, 'gy', axis=1, tiled=True)  46.5 us
    all_gather x1, waiting for transfers between devices, body(): lax.all_gather(down_weight, 'gy', axis=1, tiled=True)  43.3 us
    all_gather x1, waiting for transfers between devices, body(): lax.all_gather(merge_weight, 'gy', axis=2, tiled=True)  40.9 us
    reduce_scatter x1, waiting for transfers between devices, body(): lax.psum_scatter(down_terms.astype(jnp.bfloat16), 'gx', scatter_dimension...  38.6 us
    all_gather x1, waiting for transfers between devices, body(): full_rows = lax.all_gather(tokens, 'gx', axis=1, tiled=True)  38.4 us
    reduce_scatter x1, waiting for transfers between devices, body(): lax.psum_scatter(out_terms.astype(jnp.bfloat16), 'gx', scatter_dimension=...  38 us
  transfers between devices with their start and end apart: 10, of which 10 were waited for; matrix products, arithmetic and copies ran while one was open for 6% of the time, Pallas kernels for 0%

commit v1 on v0

--- a/solution.py
+++ b/solution.py
@@ -6,6 +6,12 @@
 HEAD = 104
 IMG_W = 16
 EPSILON = 1e-06
+
+
+def joined_along(blocks, dim):
+    blocks = jnp.moveaxis(blocks, 0, dim)
+    shape = blocks.shape
+    return blocks.reshape(*shape[:dim], shape[dim] * shape[dim + 1], *shape[dim + 2 :])
 
 
 def normalize_rows(values, gain, bias):
@@ -78,7 +84,19 @@
     tok_rows = tokens.shape[0]
     feature_cols = tokens.shape[1]
     features = feature_cols * lax.axis_size("gx")
-    full_rows = lax.all_gather(tokens, "gx", axis=1, tiled=True)
+    length = lax.axis_size("gx")
+    pairs = [(i, (i + 1) % length) for i in range(length)]
+    back = [(b, a) for a, b in pairs]
+    lower, upper_2 = ([], [])
+    for step in range(length - 1):
+        if step % 2 == 0:
+            lower.append(lax.ppermute(lower[-1] if lower else tokens, "gx", pairs))
+        else:
+            upper_2.append(lax.ppermute(upper_2[-1] if upper_2 else tokens, "gx", back))
+    pieces = jnp.stack([*lower[::-1], tokens, *upper_2])
+    shift = lax.axis_index("gx") - len(lower)
+    pieces = pieces[(jnp.arange(length) - shift) % length]
+    full_rows = joined_along(pieces, 1)
     normed = normalize_rows(full_rows, first_gain, first_bias).astype(jnp.bfloat16)
     columns = normed
     qkv = jnp.einsum(

time: 598 us -> 557 us (0.931)
  waiting for transfers between devices: 399 us -> 339 us
  local copies, waits for them, and re-layouts: 46.7 us -> 56.1 us
    all_gather x1, waiting for transfers between devices: 46.5 us -> 0.02 us  [body(): lax.all_gather(project_out, 'gy', axis=1, tiled=True)]
    ppermute x0 -> x3, waiting for transfers between devices: none -> 39.2 us  [the longest x2 39.2 us: body(): lower.append(lax.ppermute(lower[-1] if lower else tokens, 'gx', pairs))]
    all_gather x1 -> x0, waiting for transfers between devices: 38.4 us -> none  [body(): full_rows = lax.all_gather(tokens, 'gx', axis=1, tiled=True)]
    all_gather x1, waiting for transfers between devices: 47 us -> 33.3 us  [body(): lax.all_gather(query_key_value, 'gy', axis=1, tiled=True)]
    convert_element_type x0 -> x1, local copies, waits for them, and re-layouts: none -> 7.65 us  [normalize_rows(): values = values.astype(jnp.float32)]
    unnamed x32 -> x28, local copies, waits for them, and re-layouts: 24 us -> 23 us
  transfers between devices with their start and end apart: 10 -> 12, of which waited for: 10 -> 10; matrix products, arithmetic and copies ran while one was open for 6% -> 9% of each run, Pallas kernels for 0% -> 0%
where the time goes in v1:
time: 557 us; the launch traced here: 548 us
  waiting for transfers between devices  339 us (61%)
  matrix products  85.3 us (15%)
  local copies, waits for them, and re-layouts  56.1 us (10%)
  blocking collectives  26.6 us (5%)
  other arithmetic  21 us (4%)
  between operations  13.9 us (2%)
    all_gather x1, waiting for transfers between devices, body(): lax.all_gather(up_weight, 'gy', axis=0, tiled=True)  50.3 us
    all_gather x1, waiting for transfers between devices, body(): lax.all_gather(down_weight, 'gy', axis=1, tiled=True)  43.4 us
    all_gather x1, waiting for transfers between devices, body(): lax.all_gather(merge_weight, 'gy', axis=2, tiled=True)  40.9 us
    ppermute x2, waiting for transfers between devices, body(): lower.append(lax.ppermute(lower[-1] if lower else tokens, 'gx', pairs))  39.2 us
    reduce_scatter x1, waiting for transfers between devices, body(): lax.psum_scatter(down_terms.astype(jnp.bfloat16), 'gx', scatter_dimension...  38.6 us
    reduce_scatter x1, waiting for transfers between devices, body(): lax.psum_scatter(out_terms.astype(jnp.bfloat16), 'gx', scatter_dimension=...  38 us
    all_gather x1, waiting for transfers between devices, body(): lax.all_gather(query_key_value, 'gy', axis=1, tiled=True)  33.3 us
    all_gather x1, waiting for transfers between devices, body(): resid_rows = lax.all_gather(first_resid, 'gx', axis=1, tiled=True)  33.1 us
  transfers between devices with their start and end apart: 12, of which 10 were waited for; matrix products, arithmetic and copies ran while one was open for 9% of the time, Pallas kernels for 0%

profile of v1, /device:TPU:1, one launch (start us, length us, event | category | flops | bytes accessed | tf_op | source)
XLA Modules:
  0.0 548.1 jit_solution(9761542293915147499)
XLA Ops:
  13.8 18.8 %collective-permute-done = bf16[1024,416]{0,1:T(8,128)(2,1)S(1)} collective-permute-done((bf16[1024,416]{0,1:T(8,128)(2,1)}, bf16[1024,416]{0,1:T(8,128)(2,1)S(1)}, u32[]{:S(2)}, u32[]{:S(2)}) %collective-permute-start) | collective-permute-done | bytes 852000 | tf_op jit(solution)/shard_map/ppermute | solution.py:93
  32.6 20.4 %collective-permute-done.1 = bf16[1024,416]{0,1:T(8,128)(2,1)S(1)} collective-permute-done((bf16[1024,416]{0,1:T(8,128)(2,1)S(1)}, bf16[1024,416]{0,1:T(8,128)(2,1)S(1)}, u32[]{:S(2)}, u32[]{:S(2)}) %collective-permute-start.1) | collective-permute-done | bytes 852000 | tf_op jit(solution)/shard_map/ppermute | solution.py:93
  62.3 7.7 %copy.27 = f32[1024,1664]{1,0:T(8,128)} copy(f32[1024,1664]{0,1:T(8,128)} %bitcast.85) | data formatting | bytes 13631488 | tf_op jit(solution)/shard_map/convert_element_type | solution.py:18
  74.4 33.3 %all-gather.10.cloned.1.call-done = bf16[3,1664,416]{2,0,1:T(4,128)(2,1)} async-done(((bf16[3,52,416]{2,0,1:T(4,128)(2,1)}), bf16[3,1664,416]{2,0,1:T(4,128)(2,1)}) %all-gather.10.cloned.1.call-update) | async-done | bytes 4153360 | tf_op jit(solution)/shard_map/all_gather | solution.py:105
  107.6 10.7 %convert_bitcast_fusion = bf16[3,1024,416]{1,2,0:T(8,128)(2,1)S(1)} fusion(bf16[3,1664,416]{2,0,1:T(4,128)(2,1)} %all-gather.10.cloned.1.call-done, f32[1024,1664]{1,0:T(8,128)} %copy.27, f32[1664]{0:T(1024)S(1)} %copy-done.5, f32[1664]{0:T(1024)S(1)} %copy-done.6, f32[1024]{0:T(1024)S(1)} %add_rsqrt_fusion.2, f32[1024]{0:T(1024)S(1)} %broadcast_multiply_fusion.2), kind=kOutput, calls=%fused_computation.76 | convolution fusion | flops 4262821888 | bytes 13546496 | tf_op jit(solution)/shard_map/td,kdc->ktc/dot_general | solution.py:102
  119.9 30.2 %while.10 = (s32[]{:T(128)}, bf16[2,512,4,104]{1,3,2,0:T(8,128)(2,1)}, s32[2]{0:T(128)S(1)}, s32[1024]{0:T(1024)S(1)}, bf16[1024,4,104]{0,2,1:T(8,128)(2,1)}, /*...) while((s32[]{:T(128)}, ...), condition=%wide.region_8.9_spmd, body=%wide.region_5.8_spmd.sunk | while | flops 885736448 | bytes 20409008 | solution.py:64
  121.8 7.6 %fusion.153 = (f32[4,512]{1,0:T(4,128)S(1)}, f32[4,512,1024]{2,1,0:T(8,128)}) fusion(pred[512,1024]{1,0:T(8,128)(4,1)S(1)} %broadcast_compare_fusion.2, bf16[1024,4,104]{0,2,1:T(8,128)(2,1)} %get-tuple-element.142, bf16[1024,4,104]{0,2,1:T(8,128)(2,1)} %get-tuple-element.141, s32[]{:T(128)S(6)} %select_n.82), kind=kOutput, calls=%fused_computation.141.clone.1 | convolution fusion | flops 444597248 | bytes 10199044 | tf_op jit(solution)/shard_map/while/body/eval_jaxpr/sub | solution.py:58
  129.4 5.7 %fusion.154 = bf16[2,512,4,104]{1,3,2,0:T(8,128)(2,1)} fusion(bf16[2,512,4,104]{1,3,2,0:T(8,128)(2,1)} %get-tuple-element.127, s32[]{:T(128)} %get-tuple-element.126, bf16[1024,4,104]{0,2,1:T(8,128)(2,1)S(1)} %get-tuple-element.143, f32[4,512,1024]{2,1,0:T(8,128)} %get-tuple-element.113, f32[4,512]{1,0:T(4,128)S(1)} %get-tuple-element.114), kind=kOutput, calls=%fused_computation.13.clone.1 | convolution fusion | flops 440614912 | bytes 9675264 | tf_op jit(solution)/shard_map/while/body/eval_jaxpr/hqk,khe->qhe/dot_general | solution.py:60
  136.8 7.6 %fusion.153 = (f32[4,512]{1,0:T(4,128)S(1)}, f32[4,512,1024]{2,1,0:T(8,128)}) fusion(pred[512,1024]{1,0:T(8,128)(4,1)S(1)} %broadcast_compare_fusion.2, bf16[1024,4,104]{0,2,1:T(8,128)(2,1)} %get-tuple-element.142, bf16[1024,4,104]{0,2,1:T(8,128)(2,1)} %get-tuple-element.141, s32[]{:T(128)S(6)} %select_n.82), kind=kOutput, calls=%fused_computation.141.clone.1 | convolution fusion | flops 444597248 | bytes 10199044 | tf_op jit(solution)/shard_map/while/body/eval_jaxpr/sub | solution.py:58
  157.2 38.0 %reduce-scatter.4.cloned.1.call-done = bf16[1024,416]{0,1:T(8,128)(2,1)} async-done(((bf16[1024,1664]{0,1:T(8,128)(2,1)}), bf16[1024,416]{0,1:T(8,128)(2,1)}) %reduce-scatter.4.cloned.1.call-update) | async-done | bytes 851984 | tf_op jit(solution)/shard_map/reduce_scatter | solution.py:114
  197.7 50.3 %all-gather.18.cloned.1.call-done = bf16[32,52,2048]{2,1,0:T(8,128)(2,1)} async-done(((bf16[1,52,2048]{2,1,0:T(8,128)(2,1)}), bf16[32,52,2048]{2,1,0:T(8,128)(2,1)}) %all-gather.18.cloned.1.call-update) | async-done | bytes 6815760 | tf_op jit(solution)/shard_map/all_gather | solution.py:123
  248.0 8.6 %reshape.193 = bf16[1664,2048]{1,0:T(8,128)(2,1)} reshape(bf16[32,52,2048]{2,1,0:T(8,128)(2,1)} %all-gather.18.cloned.1.call-done) | data formatting | bytes 13631488
  256.5 43.4 %all-gather.20.cloned.1.call-done = bf16[32,52,2048]{2,1,0:T(8,128)(2,1)} async-done(((bf16[1,52,2048]{2,1,0:T(8,128)(2,1)}), bf16[32,52,2048]{2,1,0:T(8,128)(2,1)}) %all-gather.20.cloned.1.call-update) | async-done | bytes 6815760 | tf_op jit(solution)/shard_map/all_gather | solution.py:129
  299.9 9.0 %reshape.195 = bf16[1664,2048]{1,0:T(8,128)(2,1)} reshape(bf16[32,52,2048]{2,1,0:T(8,128)(2,1)} %all-gather.20.cloned.1.call-done) | data formatting | bytes 13631488
  308.9 33.1 %all-gather.12.cloned.1.call-done = bf16[1024,1664]{0,1:T(8,128)(2,1)} async-done(((bf16[1024,416]{0,1:T(8,128)(2,1)}), bf16[1024,1664]{0,1:T(8,128)(2,1)}) %all-gather.12.cloned.1.call-update) | async-done | bytes 3407888 | tf_op jit(solution)/shard_map/all_gather | solution.py:118
  347.8 29.2 %fusion.143 = bf16[1024,2048]{1,0:T(8,128)(2,1)S(1)} fusion(bf16[1664,2048]{1,0:T(8,128)(2,1)} %reshape.193, bf16[1024,1664]{0,1:T(8,128)(2,1)S(1)} %copy-done.1, f32[1664]{0:T(1024)S(1)} %copy-done.7, f32[1664]{0:T(1024)S(1)} %copy-done.8, f32[1024]{0:T(1024)S(1)} %add_rsqrt_fusion.1, f32[1024]{0:T(1024)S(1)} %broadcast_multiply_fusion.1), kind=kOutput, calls=%fused_computation.28.clone.clone.clone.clone.1 | convolution fusion | flops 7125860352 | bytes 14439424 | tf_op jit(solution)/shard_map/dot_general | solution.py:121
  377.1 8.7 %fusion.46 = bf16[1024,1664]{0,1:T(8,128)(2,1)} fusion(bf16[1664,2048]{1,0:T(8,128)(2,1)S(1)} %bitcast.88, bf16[1024,2048]{1,0:T(8,128)(2,1)S(1)} %fusion.143), kind=kOutput, calls=%fused_computation.57 | convolution fusion | flops 6981025792 | bytes 14417920 | tf_op jit(solution)/shard_map/dot_general | solution.py:127
  388.2 38.6 %reduce-scatter.6.cloned.1.call-done = bf16[1024,416]{0,1:T(8,128)(2,1)} async-done(((bf16[1024,1664]{0,1:T(8,128)(2,1)}), bf16[1024,416]{0,1:T(8,128)(2,1)}) %reduce-scatter.6.cloned.1.call-update) | async-done | bytes 851984 | tf_op jit(solution)/shard_map/reduce_scatter | solution.py:132
  428.3 6.6 %all-reduce = (f32[1024]{0:T(1024)S(1)}, f32[1024]{0:T(1024)S(1)}) all-reduce(f32[1024]{0:T(1024)S(1)} %get-tuple-element.44, f32[1024]{0:T(1024)S(1)} %get-tuple-element.43), channel_id=1, replica_groups=mesh['gx'=4,'gy'=32] {'gx'}, use_global_device_ids=true, to_apply=%region_16.17 | all-reduce | flops 2048 | bytes 16384 | tf_op jit(solution)/shard_map/psum | solution.py:136
  438.0 40.9 %all-gather.14.cloned.1.call-done = bf16[4,416,1664]{1,0,2:T(4,128)(2,1)} async-done(((bf16[4,416,52]{1,0,2:T(4,128)(2,1)}), bf16[4,416,1664]{1,0,2:T(4,128)(2,1)}) %all-gather.14.cloned.1.call-update) | async-done | bytes 5537808 | tf_op jit(solution)/shard_map/all_gather | solution.py:153
  478.9 6.3 %fusion.72 = bf16[256,1664]{0,1:T(8,128)(2,1)} fusion(bf16[256,4,416]{2,0,1:T(8,128)(2,1)S(1)} %bitcast.93, bf16[4,416,1664]{1,0,2:T(4,128)(2,1)} %all-gather.14.cloned.1.call-done), kind=kOutput, calls=%fused_computation.72 | convolution fusion | flops 1418100736 | bytes 7241728 | tf_op jit(solution)/shard_map/pkf,kfc->pc/dot_general | solution.py:150
  486.2 19.4 %reduce-scatter.8.cloned.1.call-done = bf16[256,416]{0,1:T(8,128)(2,1)} async-done(((bf16[256,1664]{0,1:T(8,128)(2,1)}), bf16[256,416]{0,1:T(8,128)(2,1)}) %reduce-scatter.8.cloned.1.call-update) | async-done | bytes 213008 | tf_op jit(solution)/shard_map/reduce_scatter | solution.py:156
  506.7 13.6 %scatter_fusion = bf16[32,16,416]{2,1,0:T(8,128)(2,1)S(1)} fusion(bf16[32,16,416]{2,1,0:T(8,128)(2,1)S(1)} %broadcast_in_dim.19, s32[256]{0:T(256)S(1)} %bitcast.86, bf16[256,416]{1,0:T(8,128)(2,1)S(1)} %copy.35), kind=kCustom, calls=%fused_computation.1 | custom fusion | bytes 641024 | tf_op jit(solution)/shard_map/scatter | solution.py:169
  520.3 20.0 %all_to_all.5 = bf16[32,16,416]{2,1,0:T(8,128)(2,1)S(1)} all-to-all(bf16[32,16,416]{2,1,0:T(8,128)(2,1)S(1)} %scatter_fusion), channel_id=1, replica_groups=mesh['gx'=4,'gy'=32] {'gy'}, dimensions={0} | all-to-all | bytes 851968 | tf_op jit(solution)/shard_map/all_to_all | solution.py:171
  (93 shorter events, 55.3 us)
Async XLA Ops:
  6.5 65.1 %all-gather.16.cloned.1.call-start = ((), (), s32[]{:S(2)}) async-start(), calls=%async_computation.10 | async-start | bytes 1892352 | tf_op jit(solution)/shard_map/all_gather | solution.py:111
  7.3 100.4 %all-gather.10.cloned.1.call-start = ((), (), s32[]{:S(2)}) async-start(), calls=%async_computation.4 | async-start | bytes 7028736 | tf_op jit(solution)/shard_map/all_gather | solution.py:105
  9.0 186.1 %reduce-scatter.4.cloned.1.call-start = ((), (), s32[]{:S(2)}) async-start(), calls=%async_computation.5 | async-start | bytes 4259840 | tf_op jit(solution)/shard_map/reduce_scatter | solution.py:114
  9.1 23.5 %collective-permute-start = (bf16[1024,416]{0,1:T(8,128)(2,1)}, bf16[1024,416]{0,1:T(8,128)(2,1)S(1)}, u32[]{:S(2)}, u32[]{:S(2)}) collective-permute-start(bf16[1024,416]{0,1:T(8,128)(2,1)} %param.16), channel_id=1, source_target_pairs={{0,32},{32,64},{64,96},{96,0},{1,33},{33,65},{65,97},{97,1},{2,34}... | collective-permute-start | bytes 2555912 | tf_op jit(solution)/shard_map/ppermute | solution.py:93
  11.6 21.0 %collective-permute-start.2 = (bf16[1024,416]{0,1:T(8,128)(2,1)}, bf16[1024,416]{0,1:T(8,128)(2,1)S(1)}, u32[]{:S(2)}, u32[]{:S(2)}) collective-permute-start(bf16[1024,416]{0,1:T(8,128)(2,1)} %param.16), channel_id=1, source_target_pairs={{32,0},{64,32},{96,64},{0,96},{33,1},{65,33},{97,65},{1,97},{34,2}... | collective-permute-start | bytes 2555912 | tf_op jit(solution)/shard_map/ppermute | solution.py:95
  32.6 20.5 %collective-permute-start.1 = (bf16[1024,416]{0,1:T(8,128)(2,1)S(1)}, bf16[1024,416]{0,1:T(8,128)(2,1)S(1)}, u32[]{:S(2)}, u32[]{:S(2)}) collective-permute-start(bf16[1024,416]{0,1:T(8,128)(2,1)S(1)} %collective-permute-done), channel_id=1, source_target_pairs={{0,32},{32,64},{64,96},{96,0},{1,33},{33,65},{65,97},{97,1},{2,34}... | collective-permute-start | bytes 2555912 | tf_op jit(solution)/shard_map/ppermute | solution.py:93
  70.0 37.6 %copy-start.5 = (f32[1664]{0:T(1024)S(1)}, f32[1664]{0:T(1024)}, u32[]{:S(2)}) copy-start(f32[1664]{0:T(1024)} %param.19) | copy-start | bytes 19972
  70.0 37.6 %copy-start.6 = (f32[1664]{0:T(1024)S(1)}, f32[1664]{0:T(1024)}, u32[]{:S(2)}) copy-start(f32[1664]{0:T(1024)} %param.18) | copy-start | bytes 19972
  74.3 45.5 %copy-start.3 = (s32[1024]{0:T(1024)S(1)}, s32[1024]{0:T(1024)}, u32[]{:S(2)}) copy-start(s32[1024]{0:T(1024)} %param.17) | copy-start | bytes 12292
  152.3 42.9 %copy-start.2 = (bf16[1024,416]{0,1:T(8,128)(2,1)S(1)}, bf16[1024,416]{0,1:T(8,128)(2,1)}, u32[]{:S(2)}) copy-start(bf16[1024,416]{0,1:T(8,128)(2,1)} %param.16) | copy-start | bytes 2555908
  156.0 92.0 %all-gather.18.cloned.1.call-start = ((), (), s32[]{:S(2)}) async-start(), calls=%async_computation.11 | async-start | bytes 7569408 | tf_op jit(solution)/shard_map/all_gather | solution.py:123
  156.6 143.4 %all-gather.20.cloned.1.call-start = ((), (), s32[]{:S(2)}) async-start(), calls=%async_computation.12 | async-start | bytes 7569408 | tf_op jit(solution)/shard_map/all_gather | solution.py:129
  157.1 184.8 %all-gather.12.cloned.1.call-start = ((), (), s32[]{:S(2)}) async-start(), calls=%async_computation.6 | async-start | bytes 4259840 | tf_op jit(solution)/shard_map/all_gather | solution.py:118
  197.6 229.2 %reduce-scatter.6.cloned.1.call-start = ((), (), s32[]{:S(2)}) async-start(), calls=%async_computation.7 | async-start | bytes 4259840 | tf_op jit(solution)/shard_map/reduce_scatter | solution.py:132
  308.9 38.9 %copy-start.7 = (f32[1664]{0:T(1024)S(1)}, f32[1664]{0:T(1024)}, u32[]{:S(2)}) copy-start(f32[1664]{0:T(1024)} %param.23) | copy-start | bytes 19972
  308.9 38.9 %copy-start.8 = (f32[1664]{0:T(1024)S(1)}, f32[1664]{0:T(1024)}, u32[]{:S(2)}) copy-start(f32[1664]{0:T(1024)} %param.22) | copy-start | bytes 19972
  342.0 5.9 %copy-start.1 = (bf16[1024,1664]{0,1:T(8,128)(2,1)S(1)}, bf16[1024,1664]{0,1:T(8,128)(2,1)}, u32[]{:S(2)}) copy-start(bf16[1024,1664]{0,1:T(8,128)(2,1)} %all-gather.12.cloned.1.call-done) | copy-start | bytes 10223620
  344.7 32.4 %slice-start = ((s8[6815744]{0:T(1024)(128)(4,1)}), s8[4194304]{0:T(1024)(128)(4,1)S(1)}, s32[]{:S(2)}) async-start(s8[6815744]{0:T(1024)(128)(4,1)} %bitcast.87), calls=%async_computation.13 | async-start | bytes 8388608
  347.8 29.3 %slice-start.1 = ((s8[6815744]{0:T(1024)(128)(4,1)}), s8[2621440]{0:T(1024)(128)(4,1)S(1)}, s32[]{:S(2)}) async-start(s8[6815744]{0:T(1024)(128)(4,1)} %bitcast.87), calls=%async_computation.14 | async-start | bytes 5242880
  377.1 49.7 %copy-start = (bf16[1024,416]{0,1:T(8,128)(2,1)S(1)}, bf16[1024,416]{0,1:T(8,128)(2,1)}, u32[]{:S(2)}) copy-start(bf16[1024,416]{0,1:T(8,128)(2,1)} %add_convert_fusion.2) | copy-start | bytes 2555908
  385.8 93.0 %all-gather.14.cloned.1.call-start = ((), (), s32[]{:S(2)}) async-start(), calls=%async_computation.8 | async-start | bytes 7028736 | tf_op jit(solution)/shard_map/all_gather | solution.py:153
  386.6 119.0 %reduce-scatter.8.cloned.1.call-start = ((), (), s32[]{:S(2)}) async-start(), calls=%async_computation.9 | async-start | bytes 1064960 | tf_op jit(solution)/shard_map/reduce_scatter | solution.py:156
  478.9 6.4 %copy-start.4 = (s32[256,1]{0,1:T(1,128)S(1)}, s32[256,1]{0,1:T(1,128)}, u32[]{:S(2)}) copy-start(s32[256,1]{0,1:T(1,128)} %param.29) | copy-start | bytes 3076
Sparse Core Ops, SparseCore 0:
  9.6 46.5 all-gather.15
  58.5 49.1 all-gather.9
  156.1 39.0 reduce-scatter.3
  197.3 50.6 all-gather.17
  250.1 49.7 all-gather.19
  301.4 40.4 all-gather.11
  386.0 40.7 reduce-scatter.5
  429.1 49.7 all-gather.13
  485.4 20.1 reduce-scatter.7
